TPU v7x, 32 devices: a whole 2x2x4 slice. The times are simulated.
32 devices in a mesh: shard: 4 (over y, x), ctx: 4 (over z), tp: 2 (over core).
Axes of the slice: x: 2, y: 2, z: 4, core: 2. Of those that a mesh axis runs over, the one named last changes fastest.
Arguments:
- tokens: bfloat16 [10240, 768], P(('shard', 'ctx')), may hold values from -6 to 6
- seq_lengths: int32 [4], P('shard'), may hold values from 2240 to 2560
- query_weight: bfloat16 [768, 768], P('shard', 'tp'), may hold values from -0.21875 to 0.21875
- query_bias: bfloat16 [768], P(('shard', 'tp')), may hold values from -0.59765625 to 0.59765625
- key_weight: bfloat16 [768, 768], P('shard', 'tp'), may hold values from -0.21875 to 0.21875
- value_weight: bfloat16 [768, 768], P('shard', 'tp'), may hold values from -0.21875 to 0.21875
- value_bias: bfloat16 [768], P(('shard', 'tp')), may hold values from -0.119628906 to 0.119628906
- output_weight: bfloat16 [768, 768], P('shard', 'tp'), may hold values from -6 to 6
- output_bias: bfloat16 [768], P('shard'), may hold values from -0.59765625 to 0.59765625
- attn_gain: bfloat16 [768], P('shard'), may hold values from 0.5 to 1.5
- attn_shift: bfloat16 [768], P('shard'), may hold values from -0.59765625 to 0.59765625
- inner_weight: bfloat16 [768, 3072], P('shard', 'tp'), may hold values from -0.21875 to 0.21875
- inner_bias: bfloat16 [3072], P(('shard', 'tp')), may hold values from -0.59765625 to 0.59765625
- outer_weight: bfloat16 [768, 3072], P('shard', 'tp'), may hold values from -0.109375 to 0.109375
- outer_bias: bfloat16 [768], P('shard'), may hold values from -0.59765625 to 0.59765625
- final_gain: bfloat16 [768], P('shard'), may hold values from 0.5 to 1.5
- final_shift: bfloat16 [768], P('shard'), may hold values from -0.59765625 to 0.59765625
- upstream: bfloat16 [10240, 768], P(('shard', 'ctx')), may hold values from -6 to 6
Outputs:
- layer_out: bfloat16 [10240, 768], P(('shard', 'ctx'))
- tokens_gradient: float32 [10240, 768], P(('shard', 'ctx'))
- query_weight_gradient: float32 [768, 768], P('shard', 'tp')
- query_bias_gradient: float32 [768], P(('shard', 'tp'))
- key_weight_gradient: float32 [768, 768], P('shard', 'tp')
- value_weight_gradient: float32 [768, 768], P('shard', 'tp')
- value_bias_gradient: float32 [768], P(('shard', 'tp'))
- output_weight_gradient: float32 [768, 768], P('shard', 'tp')
- output_bias_gradient: float32 [768], P('shard')
- attn_gain_gradient: float32 [768], P('shard')
- attn_shift_gradient: float32 [768], P('shard')
- inner_weight_gradient: float32 [768, 3072], P('shard', 'tp')
- inner_bias_gradient: float32 [3072], P(('shard', 'tp'))
- outer_weight_gradient: float32 [768, 3072], P('shard', 'tp')
- outer_bias_gradient: float32 [768], P('shard')
- final_gain_gradient: float32 [768], P('shard')
- final_shift_gradient: float32 [768], P('shard')
All inputs are finite; a program needn't handle non-finite values.
Results may differ from a plain program's by a relative error of at most 0.014.
Values may be sent and summed in bfloat16 or wider, within the bound.
No kernel may reach another device: no remote copies, remote signals or barrier semaphores. Data moves between devices by JAX's collectives and lax.ppermute only.
A program may use at most 128 MiB of HBM per device.

v0:
```python
import jax
import jax.numpy as jnp
from jax import lax
from jax.sharding import PartitionSpec as P

HEAD_DIM = 64
EPSILON = 1e-12


def norm_parts(hidden):
    center = hidden - jnp.mean(hidden, -1, keepdims=True)
    inverse = lax.rsqrt(jnp.mean(center * center, -1, keepdims=True) + EPSILON)
    return (center * inverse, inverse)


def norm_back(gradient, normal_form, inverse, gain):
    scaled = gradient * gain
    inner = (
        scaled
        - jnp.mean(scaled, -1, keepdims=True)
        - normal_form * jnp.mean(scaled * normal_form, -1, keepdims=True)
    )
    return (inner * inverse, jnp.sum(gradient * normal_form, 0), jnp.sum(gradient, 0))


def exact_gelu(values):
    return jax.nn.gelu(values, approximate=False)


def tp_sum(value):
    if lax.axis_size("tp") == 2:
        return value + lax.ppermute(value, "tp", [(0, 1), (1, 0)])
    return lax.psum(value, "tp")


def tp_gather(value):
    if lax.axis_size("tp") == 2:
        other = lax.ppermute(value, "tp", [(0, 1), (1, 0)])
        first = lax.axis_index("tp") == 0
        return jnp.stack([jnp.where(first, value, other), jnp.where(first, other, value)])
    return lax.all_gather(value, "tp")


def on_device(
    tokens,
    seq_lengths,
    query_weight,
    query_bias,
    key_weight,
    value_weight,
    value_bias,
    output_weight,
    output_bias,
    attn_gain,
    attn_shift,
    inner_weight,
    inner_bias,
    outer_weight,
    outer_bias,
    final_gain,
    final_shift,
    upstream,
):
    row_count, model_width = tokens.shape
    tensor_place = lax.axis_index("tp")
    tensor_count = lax.axis_size("tp")
    head_width = query_weight.shape[1]
    hidden_width = inner_weight.shape[1]
    head_count = head_width // HEAD_DIM
    factor = HEAD_DIM ** (-0.5)
    f32 = jnp.float32
    qb = query_bias.shape[0]
    ib = inner_bias.shape[0]
    piece = output_bias.shape[0]
    tp_blocks = tp_gather(jnp.concatenate([query_bias, value_bias, inner_bias]))
    bias_columns = jnp.concatenate(
        [
            tp_blocks[:, :qb].reshape(piece, 1),
            tp_blocks[:, qb : 2 * qb].reshape(piece, 1),
            tp_blocks[:, 2 * qb :].reshape(piece, -1),
        ],
        axis=1,
    )
    shard_columns = jnp.stack(
        [output_bias, attn_gain, attn_shift, outer_bias, final_gain, final_shift], axis=1
    )
    kv_vec_full = lax.all_gather(
        jnp.concatenate([key_weight, value_weight, shard_columns, bias_columns], axis=1),
        "shard",
        axis=0,
        tiled=True,
    )
    query_full = lax.all_gather(query_weight, "shard", axis=0, tiled=True)
    vector_full = kv_vec_full[:, 2 * head_width :]
    key_full = kv_vec_full[:, :head_width]
    value_full = kv_vec_full[:, head_width : 2 * head_width]
    qkv_full = jnp.concatenate([query_full, kv_vec_full[:, : 2 * head_width]], axis=1)
    rest_full = lax.all_gather(
        jnp.concatenate([output_weight, inner_weight, outer_weight], axis=1),
        "shard",
        axis=0,
        tiled=True,
    )
    output_full = rest_full[:, :head_width]
    inner_full = rest_full[:, head_width : head_width + hidden_width]
    outer_full = rest_full[:, head_width + hidden_width :]
    full_vectors = vector_full[:, :6].T.astype(f32)
    outbias_full, gain_first, shift_first, outerbias_full, gain_second, shift_second = full_vectors
    qbias_all = vector_full[:, 6]
    vbias_all = vector_full[:, 7]
    ibias_all = vector_full[:, 8:].reshape(-1)
    query_shift = lax.dynamic_slice_in_dim(qbias_all, tensor_place * head_width, head_width).astype(
        f32
    )
    value_shift = lax.dynamic_slice_in_dim(vbias_all, tensor_place * head_width, head_width).astype(
        f32
    )
    inner_shift = lax.dynamic_slice_in_dim(
        ibias_all, tensor_place * hidden_width, hidden_width
    ).astype(f32)
    projected = jnp.dot(tokens, kv_vec_full[:, : 2 * head_width], preferred_element_type=f32)
    key_local = projected[:, :head_width].astype(jnp.bfloat16)
    value_local = (projected[:, head_width:] + value_shift).astype(jnp.bfloat16)
    query = (jnp.dot(tokens, query_full, preferred_element_type=f32) + query_shift).astype(
        jnp.bfloat16
    )
    chunk_heads = 2 if head_count % 2 == 0 else 1
    chunk_width = chunk_heads * HEAD_DIM
    kv_chunks = []
    for c in range(head_count // chunk_heads):
        columns = slice(c * chunk_width, (c + 1) * chunk_width)
        outgoing = jnp.concatenate([key_local[:, columns], value_local[:, columns]], axis=1)
        kv_chunks.append(lax.all_gather(outgoing, "ctx", axis=0, tiled=True))
    keys = jnp.concatenate([chunk[:, :chunk_width] for chunk in kv_chunks], axis=1)
    values = jnp.concatenate([chunk[:, chunk_width:] for chunk in kv_chunks], axis=1)
    allowed = jnp.arange(keys.shape[0]) < seq_lengths[0]

    def split_heads_of(matrix, count):
        return matrix.reshape(matrix.shape[0], count, HEAD_DIM).transpose(1, 0, 2)

    def split_heads(matrix):
        return split_heads_of(matrix, head_count)

    def join_heads(stacked):
        return stacked.transpose(1, 0, 2).reshape(stacked.shape[1], head_width)

    def scores_of(query_head, key_head):
        scores = jnp.einsum("qd,kd->qk", query_head, key_head, preferred_element_type=f32) * factor
        return jnp.where(allowed[None, :], scores, -1e30)

    def head_forward(triple):
        query_head, key_head, value_head = triple
        scores = scores_of(query_head, key_head)
        highest = jnp.max(scores, -1, keepdims=True)
        shifted = jnp.exp(scores - highest)
        summed = jnp.sum(shifted, -1, keepdims=True)
        portion = (shifted / summed).astype(jnp.bfloat16)
        mixed = jnp.dot(portion, value_head, preferred_element_type=f32)
        return (mixed.astype(jnp.bfloat16), (highest + jnp.log(summed))[:, 0])

    query_heads = split_heads(query)
    key_heads = split_heads(keys)
    value_heads = split_heads(values)
    chunk_outs = []
    for c, chunk in enumerate(kv_chunks):
        heads = slice(c * chunk_heads, (c + 1) * chunk_heads)
        chunk_outs.append(
            lax.map(
                head_forward,
                (
                    query_heads[heads],
                    split_heads_of(chunk[:, :chunk_width], chunk_heads),
                    split_heads_of(chunk[:, chunk_width:], chunk_heads),
                ),
            )
        )
    context_heads = jnp.concatenate([o[0] for o in chunk_outs])
    log_sums = jnp.concatenate([o[1] for o in chunk_outs])
    context = join_heads(context_heads)
    attn_part = jnp.einsum("th,oh->to", context, output_full, preferred_element_type=f32)
    attended = tp_sum(attn_part) + outbias_full
    normal_first, inverse_first = norm_parts(tokens.astype(f32) + attended)
    normed = normal_first * gain_first + shift_first
    normed_low = normed.astype(jnp.bfloat16)
    hidden = jnp.dot(normed_low, inner_full, preferred_element_type=f32) + inner_shift
    active = exact_gelu(hidden).astype(jnp.bfloat16)
    branch_part = jnp.einsum("tf,of->to", active, outer_full, preferred_element_type=f32)
    branch = tp_sum(branch_part) + outerbias_full
    normal_second, inverse_second = norm_parts(normed + branch)
    layer_out = (normal_second * gain_second + shift_second).astype(jnp.bfloat16)
    dres_second, final_gain_part, final_shift_part = norm_back(
        upstream.astype(f32), normal_second, inverse_second, gain_second
    )
    dbranch = dres_second.astype(jnp.bfloat16)
    outer_bias_part = jnp.sum(dbranch.astype(f32), 0)
    outer_weight_part = jnp.einsum("to,tf->of", dbranch, active, preferred_element_type=f32)
    dactive = jnp.dot(dbranch, outer_full, preferred_element_type=f32)
    unused, gelu_pull = jax.vjp(exact_gelu, hidden)
    dhidden = gelu_pull(dactive)[0].astype(jnp.bfloat16)
    inner_weight_part = jnp.einsum("td,tf->df", normed_low, dhidden, preferred_element_type=f32)
    inner_bias_part = jnp.sum(dhidden.astype(f32), 0)
    dnormed_part = jnp.einsum("tf,df->td", dhidden, inner_full, preferred_element_type=f32)
    dnormed = dres_second + tp_sum(dnormed_part)
    dres_first, attn_gain_part, attn_shift_part = norm_back(
        dnormed, normal_first, inverse_first, gain_first
    )
    dattended = dres_first.astype(jnp.bfloat16)
    output_bias_part = jnp.sum(dattended.astype(f32), 0)
    output_weight_part = jnp.einsum("to,th->oh", dattended, context, preferred_element_type=f32)
    dcontext = jnp.dot(dattended, output_full, preferred_element_type=f32).astype(jnp.bfloat16)
    low = jnp.bfloat16
    rows = model_width
    early = jnp.concatenate(
        [
            output_weight_part,
            inner_weight_part,
            outer_weight_part,
            jnp.stack(
                [
                    output_bias_part,
                    attn_gain_part,
                    attn_shift_part,
                    outer_bias_part,
                    final_gain_part,
                    final_shift_part,
                ],
                axis=1,
            ),
            tp_gather(inner_bias_part).reshape(rows, -1),
        ],
        axis=1,
    ).astype(low)
    early_scattered = lax.psum_scatter(early, "shard", scatter_dimension=0, tiled=True)
    local_rows = piece // tensor_count

    def head_backward(quintet):
        query_head, key_head, value_head, dcontext_head, log_sum = quintet
        portion = jnp.exp(scores_of(query_head, key_head) - log_sum[:, None])
        dportion = jnp.einsum("qd,kd->qk", dcontext_head, value_head, preferred_element_type=f32)
        dvalue_head = jnp.einsum(
            "qk,qd->kd", portion.astype(jnp.bfloat16), dcontext_head, preferred_element_type=f32
        )
        centering = jnp.sum(portion * dportion, -1, keepdims=True)
        dscores = (portion * (dportion - centering)).astype(jnp.bfloat16)
        dquery_head = jnp.dot(dscores, key_head, preferred_element_type=f32) * factor
        dkey_head = (
            jnp.einsum("qk,qd->kd", dscores, query_head, preferred_element_type=f32) * factor
        )
        return (dquery_head.astype(jnp.bfloat16), dkey_head, dvalue_head)

    dquery_heads, dkey_heads, dvalue_heads = lax.map(
        head_backward, (query_heads, key_heads, value_heads, split_heads(dcontext), log_sums)
    )
    dquery = join_heads(dquery_heads)
    dkv_partial = jnp.concatenate(
        [join_heads(dkey_heads), join_heads(dvalue_heads)], axis=1
    ).astype(low)
    dkv_partial, early_scattered = lax.optimization_barrier((dkv_partial, early_scattered))
    dkv = lax.psum_scatter(dkv_partial, "ctx", scatter_dimension=0, tiled=True).astype(jnp.bfloat16)
    early_piece = lax.psum(early_scattered, "ctx").astype(f32)
    output_total = early_piece[:, :head_width]
    inner_total = early_piece[:, head_width : head_width + hidden_width]
    outer_total = early_piece[:, head_width + hidden_width : head_width + 2 * hidden_width]
    early_vectors = early_piece[:, head_width + 2 * hidden_width :]
    (
        outbias_total,
        attn_gain_total,
        attn_shift_total,
        outerbias_total,
        final_gain_total,
        final_shift_total,
    ) = early_vectors[:, :6].T
    ibias_total = lax.dynamic_slice_in_dim(
        early_vectors[:, 6:], tensor_place * local_rows, local_rows, 0
    ).reshape(-1)
    dkeys = dkv[:, :head_width]
    dvalues = dkv[:, head_width:]
    dqkv = jnp.concatenate([dquery, dkeys, dvalues], axis=1)
    qkv_weight_part = jnp.einsum("td,th->dh", tokens, dqkv, preferred_element_type=f32)
    query_bias_part = jnp.sum(dquery.astype(f32), 0)
    value_bias_part = jnp.sum(dvalues.astype(f32), 0)
    dinput_part = jnp.einsum("th,dh->td", dqkv, qkv_full, preferred_element_type=f32)
    tokens_gradient = dres_first + tp_sum(dinput_part)
    late = jnp.concatenate(
        [
            qkv_weight_part,
            tp_gather(query_bias_part).reshape(rows, 1),
            tp_gather(value_bias_part).reshape(rows, 1),
        ],
        axis=1,
    ).astype(low)
    late_piece = lax.psum(
        lax.psum_scatter(late, "shard", scatter_dimension=0, tiled=True), "ctx"
    ).astype(f32)
    query_total = late_piece[:, :head_width]
    key_total = late_piece[:, head_width : 2 * head_width]
    value_total = late_piece[:, 2 * head_width : 3 * head_width]
    qbias_total = lax.dynamic_slice_in_dim(
        late_piece[:, 3 * head_width], tensor_place * local_rows, local_rows
    )
    vbias_total = lax.dynamic_slice_in_dim(
        late_piece[:, 3 * head_width + 1], tensor_place * local_rows, local_rows
    )
    return (
        layer_out,
        tokens_gradient,
        query_total,
        qbias_total,
        key_total,
        value_total,
        vbias_total,
        output_total,
        outbias_total,
        attn_gain_total,
        attn_shift_total,
        inner_total,
        ibias_total,
        outer_total,
        outerbias_total,
        final_gain_total,
        final_shift_total,
    )


def solution(mesh):
    placed = (
        P(("shard", "ctx"), None),
        P("shard"),
        P("shard", "tp"),
        P(("shard", "tp")),
        P("shard", "tp"),
        P("shard", "tp"),
        P(("shard", "tp")),
        P("shard", "tp"),
        P("shard"),
        P("shard"),
        P("shard"),
        P("shard", "tp"),
        P(("shard", "tp")),
        P("shard", "tp"),
        P("shard"),
        P("shard"),
        P("shard"),
        P(("shard", "ctx"), None),
    )
    return jax.shard_map(
        on_device,
        mesh=mesh,
        in_specs=placed,
        out_specs=(
            P(("shard", "ctx"), None),
            P(("shard", "ctx"), None),
            P("shard", "tp"),
            P(("shard", "tp")),
            P("shard", "tp"),
            P("shard", "tp"),
            P(("shard", "tp")),
            P("shard", "tp"),
            P("shard"),
            P("shard"),
            P("shard"),
            P("shard", "tp"),
            P(("shard", "tp")),
            P("shard", "tp"),
            P("shard"),
            P("shard"),
            P("shard"),
        ),
        check_vma=False,
    )
```

profile of v0, /device:TPU:0, one launch (start us, length us, event | category | flops | bytes accessed | tf_op | source)
XLA Modules:
  0.0 627.6 jit_solution(12758260347536476679)
XLA Ops:
  16.6 31.7 %all-gather.6.cloned.1.call-done = bf16[768,780]{1,0:T(8,128)(2,1)} async-done(((bf16[192,780]{1,0:T(8,128)(2,1)}), bf16[768,780]{1,0:T(8,128)(2,1)}) %all-gather.6.cloned.1.call-update) | async-done | bytes 1198096 | tf_op jit(solution)/shard_map/all_gather | solution.py:87
  56.0 10.9 %all_gather.18 = bf16[768,384]{1,0:T(8,128)(2,1)S(1)} all-gather(bf16[192,384]{1,0:T(8,128)(2,1)S(1)} %copy-done.38), channel_id=1, replica_groups=mesh['shard'=4,'ctx'=4,'tp'=2] {'shard'}, dimensions={0}, use_global_device_ids=true | all-gather | bytes 737280 | tf_op jit(solution)/shard_map/all_gather | solution.py:93
  69.2 16.3 %all-gather.8.cloned.1.call-done = bf16[2560,256]{0,1:T(8,128)(2,1)} async-done(((bf16[640,256]{0,1:T(8,128)(2,1)}), bf16[2560,256]{0,1:T(8,128)(2,1)}) %all-gather.8.cloned.1.call-update) | async-done | bytes 1310736 | tf_op jit(solution)/shard_map/all_gather | solution.py:133
  89.2 18.7 %while.54 = (s32[]{:T(128)}, bf16[2,640,64]{1,2,0:T(8,128)(2,1)S(1)}, f32[2,640]{1,0:T(2,128)S(1)}, bf16[2,640,64]{2,1,0:T(8,128)(2,1)S(1)}, bf16[2,2560,64]{2,1...) while((s32[]{:T(128)}, ...), condition=%wide.region_3.4_spmd.clone, body=%wide.region_0.3_spmd.clone.sunk | while | flops 439134080 | bytes 50100380 | solution.py:168
  93.9 4.7 fusion.185
  103.3 4.6 fusion.185
  107.9 10.9 %all-gather.10.cloned.1.call-done = bf16[2560,256]{0,1:T(8,128)(2,1)} async-done(((bf16[640,256]{0,1:T(8,128)(2,1)}), bf16[2560,256]{0,1:T(8,128)(2,1)}) %all-gather.10.cloned.1.call-update) | async-done | bytes 1310736 | tf_op jit(solution)/shard_map/all_gather | solution.py:133
  122.4 30.0 %all-gather.12.cloned.1.call-done = bf16[2560,256]{0,1:T(8,128)(2,1)} async-done(((bf16[640,256]{0,1:T(8,128)(2,1)}), bf16[2560,256]{0,1:T(8,128)(2,1)}) %all-gather.12.cloned.1.call-update) | async-done | bytes 1310736 | tf_op jit(solution)/shard_map/all_gather | solution.py:133
  158.0 20.9 %while.55 = (s32[]{:T(128)}, bf16[2,640,64]{1,2,0:T(8,128)(2,1)S(1)}, f32[2,640]{1,0:T(2,128)S(1)}, bf16[2,640,64]{2,1,0:T(8,128)(2,1)}, bf16[2,2560,64]{2,1,0:T...) while((s32[]{:T(128)}, ...), condition=%wide.region_7.8_spmd.clone, body=%wide.region_4.7_spmd.clone.sunk | while | flops 439134080 | bytes 47478912 | solution.py:168
  164.0 4.7 fusion.189
  174.2 4.7 fusion.189
  179.6 21.3 %while.56 = (s32[]{:T(128)}, bf16[2,640,64]{1,2,0:T(8,128)(2,1)S(1)}, f32[2,640]{1,0:T(2,128)S(1)}, bf16[2,640,64]{2,1,0:T(8,128)(2,1)}, bf16[2,2560,64]{2,1,0:T...) while((s32[]{:T(128)}, ...), condition=%wide.region_11.12_spmd.clone, body=%wide.region_8.11_spmd.clone.sunk | while | flops 439134080 | bytes 50100380 | solution.py:168
  186.1 4.6 fusion.193
  196.3 4.6 fusion.193
  202.8 13.1 %all-gather.14.cloned.1.call-done = bf16[768,3456]{1,0:T(8,128)(2,1)} async-done(((bf16[192,3456]{1,0:T(8,128)(2,1)}), bf16[768,3456]{1,0:T(8,128)(2,1)}) %all-gather.14.cloned.1.call-update) | async-done | bytes 5308432 | tf_op jit(solution)/shard_map/all_gather | solution.py:98
  225.1 12.0 %multiply_convert_fusion.1 = (bf16[640,1536]{1,0:T(8,128)(2,1)S(1)}, f32[640,1536]{1,0:T(8,128)}, f32[640,1536]{1,0:T(8,128)}) fusion(f32[1536]{0:T(1024)S(1)} %dynamic-slice_convert_fusion, bf16[768,3456]{1,0:T(8,128)(2,1)S(1)} %bitcast.230, f32[640,768]{1,0:T(8,128)S(1)} %get-tuple-element.416, f32[768]{0:T(1024)S(1)} %get-tuple-element.333, ...), kind=kOutput, calls=%fused_computation.110 | convolution fusion | flops 1577287680 | bytes 14180352 | tf_op jit(solution)/shard_map/dot_general | solution.py:185
  240.3 4.2 collective-permute-done.2
  260.0 4.9 copy.92
  267.4 5.1 copy.94
  273.5 5.4 convolution_convert_fusion.2
  278.9 3.5 convolution_convert_fusion.1
  286.1 3.8 multiply_reduce_fusion.1
  293.3 8.9 %concatenate.60 = bf16[768,3466]{1,0:T(8,128)(2,1)} concatenate(bf16[768,384]{1,0:T(8,128)(2,1)S(1)} %copy.95, bf16[768,1536]{1,0:T(8,128)(2,1)S(1)} %copy-done.27, bf16[768,1536]{1,0:T(8,128)(2,1)} %convolution_convert_fusion.1, bf16[768,1]{1,0:T(8,128)(2,1)S(1)} %stack.117, bf16[768,1]{1,0:T(8,128)(2,1)S(1)} %stack.118, bf16[768,1]{1,0:T(8,128)(2,1)S(1)} %stack.119, ...), dimensions={1} | concatenate | bytes 10647552 | tf_op jit(solution)/shard_map/concatenate | solution.py:213
  307.9 85.2 %while.57 = (s32[]{:T(128)}, bf16[6,640,64]{1,2,0:T(8,128)(2,1)}, bf16[6,2560,64]{1,2,0:T(8,128)(2,1)}, bf16[6,2560,64]{1,2,0:T(8,128)(2,1)}, bf16[6,640,64]{2,1...) while((s32[]{:T(128)}, bf16[6,640,64]{1,2,0:T(8,128)(2,1)}, ...), condition=%wide.region_22.23_spmd.clone, body=%wide.region_20.22_spmd.clone.sunk | while | flops 1063569280 | bytes 53189236 | solution.py:251
  354.1 3.3 multiply_reduce_fusion.7
  393.1 4.3 pad_maximum_fusion
  397.4 6.3 copy.105
  406.1 70.1 %reduce-scatter.10.cloned.1.call-done = bf16[640,768]{1,0:T(8,128)(2,1)} async-done(((bf16[2560,768]{1,0:T(8,128)(2,1)}), bf16[640,768]{1,0:T(8,128)(2,1)}) %reduce-scatter.10.cloned.1.call-update) | async-done | bytes 983056
  480.9 7.2 %concatenate.63 = bf16[768,1154]{0,1:T(8,128)(2,1)S(1)} concatenate(bf16[768,1152]{0,1:T(8,128)(2,1)} %fusion.92, bf16[768,1]{0,1:T(2,128)(2,1)S(1)} %bitcast.233, bf16[768,1]{0,1:T(2,128)(2,1)S(1)} %bitcast.234), dimensions={1} | concatenate | bytes 3545088 | tf_op jit(solution)/shard_map/concatenate | solution.py:284
  495.1 30.1 %reduce-scatter.12.cloned.1.call-done = bf16[192,1154]{1,0:T(8,128)(2,1)} async-done(((bf16[768,1154]{1,0:T(8,128)(2,1)}), bf16[192,1154]{1,0:T(8,128)(2,1)}) %reduce-scatter.12.cloned.1.call-update) | async-done | bytes 443152
  527.3 3.8 add_add_fusion
  531.1 79.8 %all-reduce.3.cloned.1.call-done = (bf16[192,1154]{0,1:T(8,128)(2,1)}, bf16[192,3466]{1,0:T(8,128)(2,1)}) async-done(((bf16[192,1154]{0,1:T(8,128)(2,1)}, bf16[192,3466]{1,0:T(8,128)(2,1)}), (bf16[192,1154]{0,1:T(8,128)(2,1)}, bf16[192,3466]{1,0:T(8,128)(2,1)})) %all-reduce.3.cloned.1.call-update) | async-done | bytes 1774096 | tf_op jit(solution)/shard_map/psum | solution.py:292
  (356 shorter events, 218.4 us)
Async XLA Ops:
  7.2 42.4 %copy-start.24 = (bf16[640,768]{1,0:T(8,128)(2,1)S(1)}, bf16[640,768]{1,0:T(8,128)(2,1)}, u32[]{:S(2)}) copy-start(bf16[640,768]{1,0:T(8,128)(2,1)} %param.26) | copy-start | bytes 2949124
  7.2 41.1 %all-gather.6.cloned.1.call-start = ((), (), s32[]{:S(2)}) async-start(), calls=%async_computation.3 | async-start | bytes 1720320 | tf_op jit(solution)/shard_map/all_gather | solution.py:87
  8.1 5.0 collective-permute-start
  16.5 69.0 %all-gather.8.cloned.1.call-start = ((), (), s32[]{:S(2)}) async-start(), calls=%async_computation.4 | async-start | bytes 1638400 | tf_op jit(solution)/shard_map/all_gather | solution.py:133
  53.0 65.7 %all-gather.10.cloned.1.call-start = ((), (), s32[]{:S(2)}) async-start(), calls=%async_computation.5 | async-start | bytes 1638400 | tf_op jit(solution)/shard_map/all_gather | solution.py:133
  53.9 98.6 %all-gather.12.cloned.1.call-start = ((), (), s32[]{:S(2)}) async-start(), calls=%async_computation.6 | async-start | bytes 1638400 | tf_op jit(solution)/shard_map/all_gather | solution.py:133
  54.7 161.2 %all-gather.14.cloned.1.call-start = ((), (), s32[]{:S(2)}) async-start(), calls=%async_computation.7 | async-start | bytes 6635520 | tf_op jit(solution)/shard_map/all_gather | solution.py:98
  56.0 341.4 %reduce-scatter.8.cloned.1.call-start = ((), (), s32[]{:S(2)}) async-start(), calls=%async_computation.8 | async-start | bytes 6881280 | tf_op jit(solution)/shard_map/reduce_scatter | solution.py:233
  68.2 18.7 %copy-start.6 = (bf16[640,6,64]{2,0,1:T(8,128)(2,1)}, bf16[640,6,64]{2,0,1:T(8,128)(2,1)S(1)}, u32[]{:S(2)}) copy-start(bf16[640,6,64]{2,0,1:T(8,128)(2,1)S(1)} %copy.85) | copy-start | bytes 1474564
  107.9 14.6 %copy-start.31 = (bf16[2,640,64]{1,2,0:T(8,128)(2,1)}, bf16[2,640,64]{1,2,0:T(8,128)(2,1)S(1)}, u32[]{:S(2)}) copy-start(bf16[2,640,64]{1,2,0:T(8,128)(2,1)S(1)} %get-tuple-element.187) | copy-start | bytes 491524
  107.9 14.6 %copy-start.40 = (f32[2,640]{1,0:T(2,128)}, f32[2,640]{1,0:T(2,128)S(1)}, u32[]{:S(2)}) copy-start(f32[2,640]{1,0:T(2,128)S(1)} %get-tuple-element.190) | copy-start | bytes 15364
  120.1 34.5 %copy-start.16 = (bf16[2560,128]{0,1:T(8,128)(2,1)}, bf16[2560,128]{0,1:T(8,128)(2,1)S(1)}, u32[]{:S(2)}) copy-start(bf16[2560,128]{0,1:T(8,128)(2,1)S(1)} %get-tuple-element.432) | copy-start | bytes 1966084
  120.2 34.5 %copy-start.18 = (bf16[2560,128]{0,1:T(8,128)(2,1)}, bf16[2560,128]{0,1:T(8,128)(2,1)S(1)}, u32[]{:S(2)}) copy-start(bf16[2560,128]{0,1:T(8,128)(2,1)S(1)} %get-tuple-element.433) | copy-start | bytes 1966084
  200.9 17.0 %copy-start.11 = (bf16[768,780]{1,0:T(8,128)(2,1)S(1)}, bf16[768,780]{1,0:T(8,128)(2,1)}, u32[]{:S(2)}) copy-start(bf16[768,780]{1,0:T(8,128)(2,1)} %all-gather.6.cloned.1.call-done) | copy-start | bytes 3594244
  217.8 4.2 collective-permute-start.1
  219.9 5.1 slice-start.1
  240.1 4.3 collective-permute-start.2
  244.4 6.1 copy-start.46
  250.5 4.9 copy-start.8
  258.5 27.6 %collective-permute-start.3 = (f32[640,768]{1,0:T(8,128)}, f32[640,768]{1,0:T(8,128)}, u32[]{:S(2)}, u32[]{:S(2)}) collective-permute-start(f32[640,768]{1,0:T(8,128)} %fusion.102), channel_id=1, source_target_pairs={{0,1},{1,0},{2,3},{3,2},{4,5},{5,4},{6,7},{7,6},{8,9},{9,8},{10,11... | collective-permute-start | bytes 5898248 | tf_op jit(solution)/shard_map/ppermute | solution.py:32
  267.4 5.1 copy-start.41
  273.1 5.8 copy-start.9
  273.1 5.8 copy-start.43
  273.1 11.8 %collective-permute-start.4 = (bf16[1536]{0:T(1024)(128)(2,1)S(1)}, bf16[1536]{0:T(1024)(128)(2,1)S(1)}, u32[]{:S(2)}, u32[]{:S(2)}) collective-permute-start(bf16[1536]{0:T(1024)(128)(2,1)S(1)} %get-tuple-element.464), channel_id=1, source_target_pairs={{0,1},{1,0},{2,3},{3,2},{4,5},{5,4},{6,7},{7,6},{8,9},{9,8},{10,11... | collective-permute-start | bytes 9224 | tf_op jit(solution)/shard_map/ppermute | solution.py:38
  302.3 173.9 %reduce-scatter.10.cloned.1.call-start = ((), (), s32[]{:S(2)}) async-start(), calls=%async_computation.9 | async-start | bytes 4915200
  403.7 74.4 %copy-start.26 = (bf16[640,768]{1,0:T(8,128)(2,1)S(1)}, bf16[640,768]{1,0:T(8,128)(2,1)}, u32[]{:S(2)}) copy-start(bf16[640,768]{1,0:T(8,128)(2,1)} %param.26) | copy-start | bytes 2949124
  403.7 121.5 %reduce-scatter.12.cloned.1.call-start = ((), (), s32[]{:S(2)}) async-start(), calls=%async_computation.10 | async-start | bytes 2457600
  404.9 1.2 collective-permute-start.6
  477.9 2.9 collective-permute-start.7
  490.4 120.5 %all-reduce.3.cloned.1.call-start = ((), (), s32[]{:S(2)}) async-start(), calls=%async_computation.11 | async-start | bytes 3940352 | tf_op jit(solution)/shard_map/psum | solution.py:292
  494.6 32.8 %copy-start.5 = (f32[640,768]{1,0:T(8,128)S(1)}, f32[640,768]{1,0:T(8,128)}, u32[]{:S(2)}) copy-start(f32[640,768]{1,0:T(8,128)} %copy-done.3) | copy-start | bytes 5898244
  494.6 32.7 %collective-permute-start.5 = (f32[640,768]{1,0:T(8,128)}, f32[640,768]{1,0:T(8,128)}, u32[]{:S(2)}, u32[]{:S(2)}) collective-permute-start(f32[640,768]{1,0:T(8,128)} %fusion.110), channel_id=1, source_target_pairs={{0,1},{1,0},{2,3},{3,2},{4,5},{5,4},{6,7},{7,6},{8,9},{9,8},{10,11... | collective-permute-start | bytes 5898248 | tf_op jit(solution)/shard_map/ppermute | solution.py:32
  (42 other events, 113.1 us)
Sparse Core Ops, SparseCore 0:
  16.6 31.5 all-gather.5
  53.2 32.2 all-gather.7
  87.1 31.6 all-gather.9
  120.8 31.6 all-gather.11
  154.7 61.1 all-gather.13
  302.4 63.4 reduce-scatter.7
  403.8 72.3 reduce-scatter.9
  490.5 34.6 reduce-scatter.11
  528.3 82.5 all-reduce.2
where the time goes:
time: 633 us; the launch traced here: 628 us
  waiting for transfers between devices  288 us (45%)
  matrix products  155 us (24%)
  local copies, waits for them, and re-layouts  98.7 us (16%)
  other arithmetic  56.9 us (9%)
  between operations  15 us (2%)
  blocking collectives  10.9 us (2%)
    unnamed x11, waiting for transfers between devices  100 us
    psum x1, waiting for transfers between devices, on_device(): lax.psum(lax.psum_scatter(late, 'shard', scatter_dimension=0, tiled=True)...  79.8 us
    all_gather x3, waiting for transfers between devices, on_device(): kv_chunks.append(lax.all_gather(outgoing, 'ctx', axis=0, tiled=True))  57.2 us
    all_gather x1, waiting for transfers between devices, on_device(): lax.all_gather(jnp.concatenate([key_weight, value_weight, shard_columns,...  31.7 us
    dot_general x12, matrix products, scores_of(): jnp.einsum('qd,kd->qk', query_head, key_head, preferred_element_type=f32)  30.3 us
    dot_general x6, matrix products, head_forward(): mixed = jnp.dot(portion, value_head, preferred_element_type=f32)  27.8 us
    unnamed x101, local copies, waits for them, and re-layouts  21.3 us
    reshape x10, local copies, waits for them, and re-layouts, split_heads_of(): return matrix.reshape(matrix.shape[0], count, HEAD_DIM).transpose(1, 0, 2)  19.7 us
  transfers between devices with their start and end apart: 17, of which 11 were waited for; matrix products, arithmetic and copies ran while one was open for 34% of the time, Pallas kernels for 0%

commit v1 on v0

--- a/solution.py
+++ b/solution.py
@@ -5,6 +5,24 @@
 
 HEAD_DIM = 64
 EPSILON = 1e-12
+
+
+def collect(shard, axis, dim):
+    ways, here, lap = (lax.axis_size(axis), lax.axis_index(axis), shard.shape[dim])
+    lengths = [n * ways if d == dim else n for d, n in enumerate(shard.shape)]
+    full = lax.dynamic_update_slice_in_dim(
+        jnp.zeros(lengths, shard.dtype), shard, here * lap, axis=dim
+    )
+    going_up = going_down = shard
+    for far in range(1, ways // 2 + 1):
+        going_up = lax.ppermute(going_up, axis, [(d, (d + 1) % ways) for d in range(ways)])
+        full = lax.dynamic_update_slice_in_dim(full, going_up, (here - far) % ways * lap, axis=dim)
+        if 2 * far < ways:
+            going_down = lax.ppermute(going_down, axis, [(d, (d - 1) % ways) for d in range(ways)])
+            full = lax.dynamic_update_slice_in_dim(
+                full, going_down, (here + far) % ways * lap, axis=dim
+            )
+    return full
 
 
 def norm_parts(hidden):
@@ -130,7 +148,7 @@
     for c in range(head_count // chunk_heads):
         columns = slice(c * chunk_width, (c + 1) * chunk_width)
         outgoing = jnp.concatenate([key_local[:, columns], value_local[:, columns]], axis=1)
-        kv_chunks.append(lax.all_gather(outgoing, "ctx", axis=0, tiled=True))
+        kv_chunks.append(collect(outgoing, "ctx", 0))
     keys = jnp.concatenate([chunk[:, :chunk_width] for chunk in kv_chunks], axis=1)
     values = jnp.concatenate([chunk[:, chunk_width:] for chunk in kv_chunks], axis=1)
     allowed = jnp.arange(keys.shape[0]) < seq_lengths[0]

time: 633 us -> 582 us (0.919)
  waiting for transfers between devices: 288 us -> 213 us
  starting transfers between devices: 2.28 us -> 30.4 us
    all_gather x3 -> x0, waiting for transfers between devices: 57.2 us -> none  [on_device(): kv_chunks.append(lax.all_gather(outgoing, 'ctx', axis=0, tiled=True))]
    ppermute x0 -> x9, starting transfers between devices: none -> 28.3 us  [the longest x6 15.2 us: collect(): lax.ppermute(going_up, axis, [(d, (d + 1) % ways) for d in range(ways)])]
    reshape x10 -> x2, local copies, waits for them, and re-layouts: 19.7 us -> 3.18 us  [split_heads_of(): return matrix.reshape(matrix.shape[0], count, HEAD_DIM).transpose(1, 0, 2)]
    all_gather x1, waiting for transfers between devices: 31.7 us -> 16.1 us  [on_device(): lax.all_gather(jnp.concatenate([key_weight, value_weight, shard_columns,...]
    ppermute x0 -> x9, waiting for transfers between devices: none -> 13.4 us  [the longest x6 13.4 us: collect(): lax.ppermute(going_up, axis, [(d, (d + 1) % ways) for d in range(ways)])]
    all_gather x1, waiting for transfers between devices: 13.1 us -> 0.01 us  [on_device(): lax.all_gather(jnp.concatenate([output_weight, inner_weight, outer_weight...]
    dynamic_update_slice x0 -> x9, local copies, waits for them, and re-layouts: none -> 9.78 us  [the longest x6 6.98 us: collect(): lax.dynamic_update_slice_in_dim(full, going_up, (here - far) % ways * lap...]
    unnamed x11 -> x8, waiting for transfers between devices: 100 us -> 98.2 us
  transfers between devices with their start and end apart: 17 -> 23, of which waited for: 11 -> 10; matrix products, arithmetic and copies ran while one was open for 34% -> 36% of each run, Pallas kernels for 0% -> 0%
where the time goes in v1:
time: 582 us; the launch traced here: 574 us
  waiting for transfers between devices  213 us (37%)
  matrix products  149 us (26%)
  local copies, waits for them, and re-layouts  94.5 us (16%)
  other arithmetic  55.7 us (10%)
  starting transfers between devices  30.4 us (5%)
  between operations  15.3 us (3%)
  blocking collectives  15.2 us (3%)
    unnamed x8, waiting for transfers between devices  98.2 us
    psum x1, waiting for transfers between devices, on_device(): lax.psum(lax.psum_scatter(late, 'shard', scatter_dimension=0, tiled=True)...  79.7 us
    dot_general x6, matrix products, head_forward(): mixed = jnp.dot(portion, value_head, preferred_element_type=f32)  27.4 us
    dot_general x12, matrix products, scores_of(): jnp.einsum('qd,kd->qk', query_head, key_head, preferred_element_type=f32)  27.1 us
    unnamed x85, local copies, waits for them, and re-layouts  22.4 us
    dot_general x6, matrix products, head_backward(): jnp.dot(dscores, key_head, preferred_element_type=f32) * factor  16.4 us
    all_gather x1, waiting for transfers between devices, on_device(): lax.all_gather(jnp.concatenate([key_weight, value_weight, shard_columns,...  16.1 us
    all_gather x1, blocking collectives, on_device(): query_full = lax.all_gather(query_weight, 'shard', axis=0, tiled=True)  15.2 us
  transfers between devices with their start and end apart: 23, of which 10 were waited for; matrix products, arithmetic and copies ran while one was open for 36% of the time, Pallas kernels for 0%

profile of v1, /device:TPU:0, one launch (start us, length us, event | category | flops | bytes accessed | tf_op | source)
XLA Modules:
  0.0 574.1 jit_solution(2555847300912680493)
XLA Ops:
  19.1 15.2 %all_gather.9 = bf16[768,384]{1,0:T(8,128)(2,1)S(1)} all-gather(bf16[192,384]{1,0:T(8,128)(2,1)S(1)} %copy-done.33), channel_id=1, replica_groups=mesh['shard'=4,'ctx'=4,'tp'=2] {'shard'}, dimensions={0}, use_global_device_ids=true | all-gather | bytes 737280 | tf_op jit(solution)/shard_map/all_gather | solution.py:111
  34.4 16.1 %all-gather.3.cloned.1.call-done = bf16[768,780]{1,0:T(8,128)(2,1)} async-done(((bf16[192,780]{1,0:T(8,128)(2,1)}), bf16[768,780]{1,0:T(8,128)(2,1)}) %all-gather.3.cloned.1.call-update) | async-done | bytes 1198096 | tf_op jit(solution)/shard_map/all_gather | solution.py:105
  60.7 3.8 collective-permute-start.5
  68.8 7.0 %collective-permute-start.8 = (bf16[640,256]{0,1:T(8,128)(2,1)S(1)}, bf16[640,256]{0,1:T(8,128)(2,1)S(1)}, u32[]{:S(2)}, u32[]{:S(2)}) collective-permute-start(bf16[640,256]{0,1:T(8,128)(2,1)S(1)} %get-tuple-element.517), channel_id=1, source_target_pairs={{0,6},{2,0},{4,2},{6,4},{1,7},{3,1},{5,3},{7,5},{8,14},{10,8},{12,... | collective-permute-start | bytes 983048 | tf_op jit(solution)/shard_map/ppermute | solution.py:21
  76.8 4.6 collective-permute-done.4
  81.3 5.1 collective-permute-start.3
  88.2 7.3 %collective-permute-done.7 = bf16[640,256]{0,1:T(8,128)(2,1)} collective-permute-done((bf16[640,256]{0,1:T(8,128)(2,1)S(1)}, bf16[640,256]{0,1:T(8,128)(2,1)}, u32[]{:S(2)}, u32[]{:S(2)}) %collective-permute-start.7) | collective-permute-done | bytes 327712 | tf_op jit(solution)/shard_map/ppermute | solution.py:18
  95.4 4.9 collective-permute-start.6
  101.3 3.7 collective-permute-start.9
  110.1 20.7 %while.54 = (s32[]{:T(128)}, bf16[2,640,64]{1,2,0:T(8,128)(2,1)S(1)}, f32[2,640]{1,0:T(2,128)}, bf16[2,640,64]{2,1,0:T(8,128)(2,1)S(1)}, bf16[2,2560,64]{1,2,0:T...) while((s32[]{:T(128)}, ...), condition=%wide.region_3.4_spmd.clone, body=%wide.region_0.3_spmd.clone.sunk | while | flops 439134080 | bytes 46823552 | solution.py:186
  115.9 4.6 fusion.185
  126.3 4.6 fusion.185
  137.3 20.2 %while.55 = (s32[]{:T(128)}, bf16[2,640,64]{1,2,0:T(8,128)(2,1)S(1)}, f32[2,640]{1,0:T(2,128)S(1)}, bf16[2,640,64]{2,1,0:T(8,128)(2,1)}, bf16[2,2560,64]{1,2,0:T...) while((s32[]{:T(128)}, ...), condition=%wide.region_7.8_spmd.clone, body=%wide.region_4.7_spmd.clone.sunk | while | flops 439134080 | bytes 49445020 | solution.py:186
  142.9 4.6 fusion.189
  152.9 4.6 fusion.189
  158.3 18.4 %while.56 = (s32[]{:T(128)}, bf16[2,640,64]{1,2,0:T(8,128)(2,1)S(1)}, f32[2,640]{1,0:T(2,128)S(1)}, bf16[2,640,64]{2,1,0:T(8,128)(2,1)S(1)}, bf16[2,2560,64]{1,2...) while((s32[]{:T(128)}, ...), condition=%wide.region_11.12_spmd.clone, body=%wide.region_8.11_spmd.clone.sunk | while | flops 439134080 | bytes 46823552 | solution.py:186
  163.0 4.6 fusion.193
  172.1 4.6 fusion.193
  186.7 12.2 %multiply_convert_fusion.1 = (bf16[640,1536]{1,0:T(8,128)(2,1)S(1)}, f32[640,1536]{1,0:T(8,128)}, f32[640,1536]{1,0:T(8,128)}) fusion(f32[1536]{0:T(1024)S(1)} %dynamic-slice_convert_fusion, bf16[768,3456]{1,0:T(8,128)(2,1)S(1)} %bitcast.244, f32[640,768]{1,0:T(8,128)S(1)} %get-tuple-element.478, f32[768]{0:T(1024)S(1)} %get-tuple-element.395, ...), kind=kOutput, calls=%fused_computation.110 | convolution fusion | flops 1577287680 | bytes 14180352 | tf_op jit(solution)/shard_map/dot_general | solution.py:203
  202.0 4.2 collective-permute-done.11
  226.1 3.8 convolution_convert_fusion.2
  229.9 3.5 convolution_convert_fusion.1
  237.2 3.8 multiply_reduce_fusion.1
  244.6 8.9 %concatenate.60 = bf16[768,3466]{1,0:T(8,128)(2,1)} concatenate(bf16[768,384]{1,0:T(8,128)(2,1)S(1)} %copy.87, bf16[768,1536]{1,0:T(8,128)(2,1)S(1)} %copy-done.26, bf16[768,1536]{1,0:T(8,128)(2,1)} %convolution_convert_fusion.1, bf16[768,1]{1,0:T(8,128)(2,1)S(1)} %stack.117, bf16[768,1]{1,0:T(8,128)(2,1)S(1)} %stack.118, bf16[768,1]{1,0:T(8,128)(2,1)S(1)} %stack.119, ...), dimensions={1} | concatenate | bytes 10647552 | tf_op jit(solution)/shard_map/concatenate | solution.py:231
  259.3 82.3 %while.57 = (s32[]{:T(128)}, bf16[6,640,64]{1,2,0:T(8,128)(2,1)}, bf16[6,2560,64]{1,2,0:T(8,128)(2,1)}, bf16[6,2560,64]{1,2,0:T(8,128)(2,1)}, bf16[6,640,64]{2,1...) while((s32[]{:T(128)}, bf16[6,640,64]{1,2,0:T(8,128)(2,1)}, ...), condition=%wide.region_22.23_spmd.clone, body=%wide.region_20.22_spmd.clone.sunk | while | flops 1063569280 | bytes 52206196 | solution.py:269
  341.6 4.2 pad_maximum_fusion
  345.8 6.3 %copy.97 = bf16[2560,768]{1,0:T(8,128)(2,1)} copy(bf16[2560,768]{0,1:T(8,128)(2,1)} %pad_maximum_fusion) | data formatting | bytes 7864320
  354.6 68.0 %reduce-scatter.10.cloned.1.call-done = bf16[640,768]{1,0:T(8,128)(2,1)} async-done(((bf16[2560,768]{1,0:T(8,128)(2,1)}), bf16[640,768]{1,0:T(8,128)(2,1)}) %reduce-scatter.10.cloned.1.call-update) | async-done | bytes 983056
  427.2 7.2 %concatenate.63 = bf16[768,1154]{0,1:T(8,128)(2,1)S(1)} concatenate(bf16[768,1152]{0,1:T(8,128)(2,1)} %fusion.92, bf16[768,1]{0,1:T(2,128)(2,1)S(1)} %bitcast.247, bf16[768,1]{0,1:T(2,128)(2,1)S(1)} %bitcast.248), dimensions={1} | concatenate | bytes 3545088 | tf_op jit(solution)/shard_map/concatenate | solution.py:302
  441.4 30.1 %reduce-scatter.12.cloned.1.call-done = bf16[192,1154]{1,0:T(8,128)(2,1)} async-done(((bf16[768,1154]{1,0:T(8,128)(2,1)}), bf16[192,1154]{1,0:T(8,128)(2,1)}) %reduce-scatter.12.cloned.1.call-update) | async-done | bytes 443152
  473.7 3.8 add_add_fusion
  477.5 79.7 %all-reduce.3.cloned.1.call-done = (bf16[192,1154]{0,1:T(8,128)(2,1)}, bf16[192,3466]{1,0:T(8,128)(2,1)}) async-done(((bf16[192,1154]{0,1:T(8,128)(2,1)}, bf16[192,3466]{1,0:T(8,128)(2,1)}), (bf16[192,1154]{0,1:T(8,128)(2,1)}, bf16[192,3466]{1,0:T(8,128)(2,1)})) %all-reduce.3.cloned.1.call-update) | async-done | bytes 1774096 | tf_op jit(solution)/shard_map/psum | solution.py:310
  (349 shorter events, 227.4 us)
Async XLA Ops:
  7.2 43.3 %all-gather.3.cloned.1.call-start = ((), (), s32[]{:S(2)}) async-start(), calls=%async_computation.3 | async-start | bytes 1720320 | tf_op jit(solution)/shard_map/all_gather | solution.py:105
  8.0 5.0 collective-permute-start
  16.4 35.4 %copy-start.17 = (bf16[640,768]{1,0:T(8,128)(2,1)S(1)}, bf16[640,768]{1,0:T(8,128)(2,1)}, u32[]{:S(2)}) copy-start(bf16[640,768]{1,0:T(8,128)(2,1)} %param.26) | copy-start | bytes 2949124
  16.4 161.1 %all-gather.5.cloned.1.call-start = ((), (), s32[]{:S(2)}) async-start(), calls=%async_computation.4 | async-start | bytes 6635520 | tf_op jit(solution)/shard_map/all_gather | solution.py:116
  19.0 326.8 %reduce-scatter.8.cloned.1.call-start = ((), (), s32[]{:S(2)}) async-start(), calls=%async_computation.5 | async-start | bytes 6881280 | tf_op jit(solution)/shard_map/reduce_scatter | solution.py:251
  34.4 30.2 %copy-start.30 = (bf16[768,384]{1,0:T(8,128)(2,1)}, bf16[768,384]{1,0:T(8,128)(2,1)S(1)}, u32[]{:S(2)}) copy-start(bf16[768,384]{1,0:T(8,128)(2,1)S(1)} %all_gather.9) | copy-start | bytes 1769476
  54.7 14.1 %collective-permute-start.1 = (bf16[640,256]{0,1:T(8,128)(2,1)S(1)}, bf16[640,256]{0,1:T(8,128)(2,1)}, u32[]{:S(2)}, u32[]{:S(2)}) collective-permute-start(bf16[640,256]{0,1:T(8,128)(2,1)S(1)} %get-tuple-element.513), channel_id=1, source_target_pairs={{0,2},{2,4},{4,6},{6,0},{1,3},{3,5},{5,7},{7,1},{8,10},{10,12},{12... | collective-permute-start | bytes 983048 | tf_op jit(solution)/shard_map/ppermute | solution.py:18
  56.2 45.1 %collective-permute-start.2 = (bf16[640,256]{0,1:T(8,128)(2,1)S(1)}, bf16[640,256]{0,1:T(8,128)(2,1)}, u32[]{:S(2)}, u32[]{:S(2)}) collective-permute-start(bf16[640,256]{0,1:T(8,128)(2,1)S(1)} %get-tuple-element.513), channel_id=1, source_target_pairs={{0,6},{2,0},{4,2},{6,4},{1,7},{3,1},{5,3},{7,5},{8,14},{10,8},{12,... | collective-permute-start | bytes 983048 | tf_op jit(solution)/shard_map/ppermute | solution.py:21
  60.7 20.7 %collective-permute-start.4 = (bf16[640,256]{0,1:T(8,128)(2,1)}, bf16[640,256]{0,1:T(8,128)(2,1)}, u32[]{:S(2)}, u32[]{:S(2)}) collective-permute-start(bf16[640,256]{0,1:T(8,128)(2,1)} %get-tuple-element.515), channel_id=1, source_target_pairs={{0,2},{2,4},{4,6},{6,0},{1,3},{3,5},{5,7},{7,1},{8,10},{10,12},{12... | collective-permute-start | bytes 983048 | tf_op jit(solution)/shard_map/ppermute | solution.py:18
  60.7 45.3 %collective-permute-start.5 = (bf16[640,256]{0,1:T(8,128)(2,1)}, bf16[640,256]{0,1:T(8,128)(2,1)}, u32[]{:S(2)}, u32[]{:S(2)}) collective-permute-start(bf16[640,256]{0,1:T(8,128)(2,1)} %get-tuple-element.515), channel_id=1, source_target_pairs={{0,6},{2,0},{4,2},{6,4},{1,7},{3,1},{5,3},{7,5},{8,14},{10,8},{12,... | collective-permute-start | bytes 983048 | tf_op jit(solution)/shard_map/ppermute | solution.py:21
  67.6 9.2 %copy-start.8 = (bf16[640,6,64]{2,0,1:T(8,128)(2,1)}, bf16[640,6,64]{2,0,1:T(8,128)(2,1)S(1)}, u32[]{:S(2)}) copy-start(bf16[640,6,64]{2,0,1:T(8,128)(2,1)S(1)} %copy.77) | copy-start | bytes 1474564
  67.8 27.7 %collective-permute-start.7 = (bf16[640,256]{0,1:T(8,128)(2,1)S(1)}, bf16[640,256]{0,1:T(8,128)(2,1)}, u32[]{:S(2)}, u32[]{:S(2)}) collective-permute-start(bf16[640,256]{0,1:T(8,128)(2,1)S(1)} %get-tuple-element.517), channel_id=1, source_target_pairs={{0,2},{2,4},{4,6},{6,0},{1,3},{3,5},{5,7},{7,1},{8,10},{10,12},{12... | collective-permute-start | bytes 983048 | tf_op jit(solution)/shard_map/ppermute | solution.py:18
  68.8 39.0 %collective-permute-start.8 = (bf16[640,256]{0,1:T(8,128)(2,1)S(1)}, bf16[640,256]{0,1:T(8,128)(2,1)S(1)}, u32[]{:S(2)}, u32[]{:S(2)}) collective-permute-start(bf16[640,256]{0,1:T(8,128)(2,1)S(1)} %get-tuple-element.517), channel_id=1, source_target_pairs={{0,6},{2,0},{4,2},{6,4},{1,7},{3,1},{5,3},{7,5},{8,14},{10,8},{12,... | collective-permute-start | bytes 983048 | tf_op jit(solution)/shard_map/ppermute | solution.py:21
  81.3 28.0 %collective-permute-start.3 = (bf16[640,256]{0,1:T(8,128)(2,1)}, bf16[640,256]{0,1:T(8,128)(2,1)S(1)}, u32[]{:S(2)}, u32[]{:S(2)}) collective-permute-start(bf16[640,256]{0,1:T(8,128)(2,1)} %collective-permute-done.1), channel_id=1, source_target_pairs={{0,2},{2,4},{4,6},{6,0},{1,3},{3,5},{5,7},{7,1},{8,10},{10,12},{12... | collective-permute-start | bytes 983048 | tf_op jit(solution)/shard_map/ppermute | solution.py:18
  95.4 35.5 %collective-permute-start.6 = (bf16[640,256]{0,1:T(8,128)(2,1)}, bf16[640,256]{0,1:T(8,128)(2,1)}, u32[]{:S(2)}, u32[]{:S(2)}) collective-permute-start(bf16[640,256]{0,1:T(8,128)(2,1)} %collective-permute-done.4), channel_id=1, source_target_pairs={{0,2},{2,4},{4,6},{6,0},{1,3},{3,5},{5,7},{7,1},{8,10},{10,12},{12... | collective-permute-start | bytes 983048 | tf_op jit(solution)/shard_map/ppermute | solution.py:18
  101.3 34.0 %collective-permute-start.9 = (bf16[640,256]{0,1:T(8,128)(2,1)}, bf16[640,256]{0,1:T(8,128)(2,1)}, u32[]{:S(2)}, u32[]{:S(2)}) collective-permute-start(bf16[640,256]{0,1:T(8,128)(2,1)} %collective-permute-done.7), channel_id=1, source_target_pairs={{0,2},{2,4},{4,6},{6,0},{1,3},{3,5},{5,7},{7,1},{8,10},{10,12},{12... | collective-permute-start | bytes 983048 | tf_op jit(solution)/shard_map/ppermute | solution.py:18
  137.3 20.9 %copy-start.15 = (bf16[2,640,64]{2,1,0:T(8,128)(2,1)S(1)}, bf16[2,640,64]{2,1,0:T(8,128)(2,1)}, u32[]{:S(2)}) copy-start(bf16[2,640,64]{2,1,0:T(8,128)(2,1)} %get-tuple-element.746) | copy-start | bytes 491524
  137.3 20.9 %copy-start.24 = (bf16[2560,128]{0,1:T(8,128)(2,1)S(1)}, bf16[2560,128]{0,1:T(8,128)(2,1)}, u32[]{:S(2)}) copy-start(bf16[2560,128]{0,1:T(8,128)(2,1)} %get-tuple-element.496) | copy-start | bytes 1966084
  158.2 18.4 %copy-start.29 = (bf16[2,640,64]{1,2,0:T(8,128)(2,1)S(1)}, bf16[2,640,64]{1,2,0:T(8,128)(2,1)}, u32[]{:S(2)}) copy-start(bf16[2,640,64]{1,2,0:T(8,128)(2,1)} %copy-done.28) | copy-start | bytes 491524
  179.5 4.2 collective-permute-start.10
  201.9 4.3 collective-permute-start.11
  213.1 16.9 %copy-start.10 = (f32[640,768]{1,0:T(8,128)}, f32[640,768]{1,0:T(8,128)S(1)}, u32[]{:S(2)}) copy-start(f32[640,768]{1,0:T(8,128)S(1)} %get-tuple-element.469) | copy-start | bytes 5898244
  221.5 15.7 %collective-permute-start.12 = (f32[640,768]{1,0:T(8,128)}, f32[640,768]{1,0:T(8,128)}, u32[]{:S(2)}, u32[]{:S(2)}) collective-permute-start(f32[640,768]{1,0:T(8,128)} %fusion.102), channel_id=1, source_target_pairs={{0,1},{1,0},{2,3},{3,2},{4,5},{5,4},{6,7},{7,6},{8,9},{9,8},{10,11... | collective-permute-start | bytes 5898248 | tf_op jit(solution)/shard_map/ppermute | solution.py:50
  225.7 10.2 %collective-permute-start.13 = (bf16[1536]{0:T(1024)(128)(2,1)S(1)}, bf16[1536]{0:T(1024)(128)(2,1)S(1)}, u32[]{:S(2)}, u32[]{:S(2)}) collective-permute-start(bf16[1536]{0:T(1024)(128)(2,1)S(1)} %get-tuple-element.532), channel_id=1, source_target_pairs={{0,1},{1,0},{2,3},{3,2},{4,5},{5,4},{6,7},{7,6},{8,9},{9,8},{10,11... | collective-permute-start | bytes 9224 | tf_op jit(solution)/shard_map/ppermute | solution.py:56
  253.5 169.0 %reduce-scatter.10.cloned.1.call-start = ((), (), s32[]{:S(2)}) async-start(), calls=%async_computation.6 | async-start | bytes 4915200
  352.1 72.2 %copy-start.19 = (bf16[640,768]{1,0:T(8,128)(2,1)S(1)}, bf16[640,768]{1,0:T(8,128)(2,1)}, u32[]{:S(2)}) copy-start(bf16[640,768]{1,0:T(8,128)(2,1)} %param.26) | copy-start | bytes 2949124
  352.1 119.4 %reduce-scatter.12.cloned.1.call-start = ((), (), s32[]{:S(2)}) async-start(), calls=%async_computation.7 | async-start | bytes 2457600
  353.4 1.2 collective-permute-start.15
  424.3 2.9 collective-permute-start.16
  436.8 120.4 %all-reduce.3.cloned.1.call-start = ((), (), s32[]{:S(2)}) async-start(), calls=%async_computation.8 | async-start | bytes 3940352 | tf_op jit(solution)/shard_map/psum | solution.py:310
  440.9 32.8 %copy-start.5 = (f32[640,768]{1,0:T(8,128)S(1)}, f32[640,768]{1,0:T(8,128)}, u32[]{:S(2)}) copy-start(f32[640,768]{1,0:T(8,128)} %copy-done.3) | copy-start | bytes 5898244
  440.9 32.7 %collective-permute-start.14 = (f32[640,768]{1,0:T(8,128)}, f32[640,768]{1,0:T(8,128)}, u32[]{:S(2)}, u32[]{:S(2)}) collective-permute-start(f32[640,768]{1,0:T(8,128)} %fusion.110), channel_id=1, source_target_pairs={{0,1},{1,0},{2,3},{3,2},{4,5},{5,4},{6,7},{7,6},{8,9},{9,8},{10,11... | collective-permute-start | bytes 5898248 | tf_op jit(solution)/shard_map/ppermute | solution.py:50
  (38 other events, 107.4 us)
Sparse Core Ops, SparseCore 0:
  16.6 33.9 all-gather.2
  52.9 61.8 all-gather.4
  253.7 61.5 reduce-scatter.7
  352.3 70.2 reduce-scatter.9
  436.9 34.6 reduce-scatter.11
  474.5 82.6 all-reduce.2
